TPU v7x, 32 devices: a whole 2x2x4 slice. The times are simulated.
32 devices in a mesh: dp: 8 (over y, x, core), mp: 4 (over z).
Axes of the slice: x: 2, y: 2, z: 4, core: 2. Of those that a mesh axis runs over, the one named last changes fastest.
Arguments:
- activations: bfloat16 [4, 16, 1024, 4096], P(None, 'dp', 'mp'), may hold values from -6 to 6
- cotangents: bfloat16 [4, 16, 1024, 4096], P(None, 'dp', 'mp'), may hold values from -0.1875 to 0.1875
- lengths: int32 [16], P('dp'), may hold values from 128 to 1024, as said below
- project_in: bfloat16 [4, 64, 4096], replicated, may hold values from -0.09375 to 0.09375
- project_out: bfloat16 [4, 64, 4096], replicated, may hold values from -0.09375 to 0.09375
- preconditioner: bfloat16 [16384, 4096], P('mp', 'dp'), as said below
- queries: bfloat16 [8192, 16384], P('dp', 'mp'), may hold values from -0.0625 to 0.0625
Outputs:
- scores: float32 [16, 8192], P(None, ('dp', 'mp'))
Inputs may be any that keep to these rules, and one draw needn't show every extreme that they name: `lengths`: positions at or past an example's length are padding; some example has all 1024 positions live. `preconditioner`: each layer's 4096 x 4096 block is symmetric.
All inputs are finite; a program needn't handle non-finite values.
Results may differ from a plain program's by a relative error of at most 0.005.
Values may be sent and summed in bfloat16 or wider, within the bound.
No kernel may reach another device: no remote copies, remote signals or barrier semaphores. Data moves between devices by JAX's collectives and lax.ppermute only.
A program may use at most 128 MiB of HBM per device.

v0:
```python
import jax
import jax.numpy as jnp
from jax import lax
from jax.sharding import PartitionSpec as P


def split_parts(dense):
    upper = dense.astype(jnp.bfloat16)
    kept = lax.optimization_barrier(upper)
    lower = (dense - kept.astype(jnp.float32)).astype(jnp.bfloat16)
    return (upper, lower)


def body(activations, cotangents, lengths, project_in, project_out, preconditioner, queries):
    width_mp = lax.axis_size("mp")
    layer_count = activations.shape[0]
    tokens_here = activations.shape[2]
    factor_size = project_in.shape[1]
    block_size = factor_size * factor_size
    group_size = width_mp // layer_count
    mp_place = lax.axis_index("mp")
    contract = (((1,), (1,)), ((), ()))
    positions = mp_place * tokens_here + jnp.arange(tokens_here, dtype=jnp.int32)
    live_mask = positions[None, :] < lengths[:, None]
    left_factor = jnp.einsum(
        "lesd,lkd->lesk", activations, project_in, preferred_element_type=jnp.float32
    ).astype(jnp.bfloat16)
    right_factor = jnp.einsum(
        "lesd,lkd->lesk", cotangents, project_out, preferred_element_type=jnp.float32
    )
    right_factor = jnp.where(live_mask[None, :, :, None], right_factor, 0.0).astype(jnp.bfloat16)
    partial_grad = jnp.einsum(
        "lesj,lesc->eljc", right_factor, left_factor, preferred_element_type=jnp.float32
    )
    partial_grad = partial_grad.reshape(partial_grad.shape[0], layer_count * block_size)
    grad_total = lax.psum(partial_grad, "mp")
    layer_place = mp_place // group_size
    grad_layer = lax.dynamic_slice_in_dim(
        grad_total, layer_place * block_size, block_size, 1
    ).astype(jnp.bfloat16)
    spread = lax.all_to_all(grad_layer, "dp", split_axis=1, concat_axis=0, tiled=True)
    partial_pre = lax.dot_general(
        spread, preconditioner, contract, preferred_element_type=jnp.float32
    )
    precond_grad = lax.psum(partial_pre, "dp")
    upper_grad, lower_grad = split_parts(precond_grad)
    scores = lax.psum_scatter(
        lax.dot_general(queries, upper_grad, contract, preferred_element_type=jnp.float32)
        + lax.dot_general(queries, lower_grad, contract, preferred_element_type=jnp.float32),
        "mp",
        scatter_dimension=0,
        tiled=True,
    )
    return scores.T


def solution(mesh):
    return jax.shard_map(
        body,
        mesh=mesh,
        in_specs=(
            P(None, "dp", "mp", None),
            P(None, "dp", "mp", None),
            P("dp"),
            P(),
            P(),
            P("mp", "dp"),
            P("dp", "mp"),
        ),
        out_specs=P(None, ("dp", "mp")),
        check_vma=False,
    )
```

profile of v0, /device:TPU:0, one launch (start us, length us, event | category | flops | bytes accessed | tf_op | source)
XLA Modules:
  0.0 151.0 jit_solution(13580495785346025847)
XLA Ops:
  6.5 0.0 copy-start
  6.5 0.0 all-reduce.3.cloned.1.call-start
  6.5 0.9 broadcast_compare_fusion
  7.4 0.7 copy-done
  8.1 8.8 %fusion.16 = bf16[4,2,256,64]{2,3,0,1:T(8,128)(2,1)S(1)} fusion(bf16[4,64,4096]{2,1,0:T(8,128)(2,1)S(1)} %copy-done, bf16[4,2,256,4096]{3,2,1,0:T(8,128)(2,1)} %param.8, pred[2,256]{1,0:T(4,128)(4,1)S(1)} %broadcast_compare_fusion), kind=kOutput, calls=%fused_computation.8 | convolution fusion | flops 1074003968 | bytes 19137024 | tf_op jit(solution)/shard_map/lesd,lkd->lesk/dot_general | solution.py:28
  16.9 9.3 %fusion.24 = f32[2,4,64,64]{3,2,1,0:T(8,128)S(1)} fusion(bf16[4,2,256,64]{2,3,0,1:T(8,128)(2,1)S(1)} %fusion.16, bf16[4,64,4096]{2,1,0:T(8,128)(2,1)} %param.10, bf16[4,2,256,4096]{3,2,1,0:T(8,128)(2,1)} %param.7), kind=kOutput, calls=%fused_computation.11 | convolution fusion | flops 1090650112 | bytes 19267584 | tf_op jit(solution)/shard_map/lesj,lesc->eljc/dot_general | solution.py:32
  26.2 0.1 reshape.40
  26.3 23.0 %all-reduce.4 = bf16[2,16384]{1,0:T(2,128)(2,1)S(1)} all-reduce(f32[2,16384]{1,0:T(2,128)S(1)} %reshape.40), channel_id=1, replica_groups=mesh['dp'=8,'mp'=4] {'mp'}, use_global_device_ids=true, to_apply=%region_0.1 | all-reduce | flops 32768 | bytes 196608 | tf_op jit(solution)/shard_map/psum | solution.py:36
  49.4 8.3 %all_to_all.19 = bf16[2,8,512]{2,0,1:T(2,128)(2,1)S(1)} all-to-all(bf16[2,8,512]{2,0,1:T(2,128)(2,1)S(1)} %bitcast.27), channel_id=1, replica_groups=mesh['dp'=8,'mp'=4] {'dp'}, dimensions={1} | all-to-all | bytes 32768 | tf_op jit(solution)/shard_map/all_to_all | solution.py:41
  57.7 4.1 %fusion.27 = f32[16,4096]{1,0:T(8,128)} fusion(bf16[16,512]{1,0:T(8,128)(2,1)S(1)} %all_to_all.17, bf16[4096,512]{1,0:T(8,128)(2,1)} %param.12), kind=kOutput, calls=%fused_computation.16 | convolution fusion | flops 67108864 | bytes 4472832 | tf_op jit(solution)/shard_map/dot_general | solution.py:42
  61.7 0.0 all-reduce.3.cloned.1.call-update
  61.8 0.0 reduce-scatter.2.cloned.1.call-start
  61.8 50.5 %all-reduce.3.cloned.1.call-done = f32[16,4096]{1,0:T(8,128)} async-done(((f32[16,4096]{1,0:T(8,128)}), f32[16,4096]{1,0:T(8,128)}) %all-reduce.3.cloned.1.call-update) | async-done | bytes 262160 | tf_op jit(solution)/shard_map/psum | solution.py:45
  112.3 0.0 copy-start.1
  112.3 1.0 convert_element_type.21
  113.3 5.6 %fusion.28 = f32[16,1024]{1,0:T(8,128)S(1)} fusion(bf16[16,4096]{1,0:T(8,128)(2,1)S(1)} %convert_element_type.21, bf16[1024,4096]{1,0:T(8,128)(2,1)} %param.13), kind=kOutput, calls=%fused_computation.17 | convolution fusion | flops 134217728 | bytes 8585216 | tf_op jit(solution)/shard_map/dot_general | solution.py:48
  119.0 0.0 copy-done.1
  119.0 6.3 %fusion.21 = f32[1024,16]{0,1:T(8,128)} fusion(f32[16,1024]{1,0:T(8,128)S(1)} %fusion.28, bf16[1024,4096]{1,0:T(8,128)(2,1)} %param.13, f32[16,4096]{1,0:T(8,128)S(1)} %copy-done.1, bf16[16,4096]{1,0:T(8,128)(2,1)S(1)} %convert_element_type.21), kind=kOutput, calls=%fused_computation.10 | convolution fusion | flops 134430720 | bytes 8912896 | tf_op jit(solution)/shard_map/dot_general | solution.py:49
  125.3 0.0 reduce-scatter.2.cloned.1.call-update
  125.3 18.9 %reduce-scatter.2.cloned.1.call-done = f32[256,16]{0,1:T(8,128)} async-done(((f32[1024,16]{0,1:T(8,128)}), f32[256,16]{0,1:T(8,128)}) %reduce-scatter.2.cloned.1.call-update) | async-done | bytes 16400 | tf_op jit(solution)/shard_map/reduce_scatter | solution.py:47
  (3 shorter events, 0.0 us)
Async XLA Ops:
  6.5 1.6 %copy-start = (bf16[4,64,4096]{2,1,0:T(8,128)(2,1)S(1)}, bf16[4,64,4096]{2,1,0:T(8,128)(2,1)}, u32[]{:S(2)}) copy-start(bf16[4,64,4096]{2,1,0:T(8,128)(2,1)} %param.11) | copy-start | bytes 6291460
  6.5 105.8 %all-reduce.3.cloned.1.call-start = ((), (), s32[]{:S(2)}) async-start(), calls=%async_computation.2 | async-start | bytes 524288 | tf_op jit(solution)/shard_map/psum | solution.py:45
  61.8 82.4 %reduce-scatter.2.cloned.1.call-start = ((), (), s32[]{:S(2)}) async-start(), calls=%async_computation.3 | async-start | bytes 81920 | tf_op jit(solution)/shard_map/reduce_scatter | solution.py:47
  112.3 6.7 %copy-start.1 = (f32[16,4096]{1,0:T(8,128)S(1)}, f32[16,4096]{1,0:T(8,128)}, u32[]{:S(2)}) copy-start(f32[16,4096]{1,0:T(8,128)} %all-reduce.3.cloned.1.call-done) | copy-start | bytes 786436
Sparse Core Ops, SparseCore 0:
  61.9 50.3 all-reduce.2
  125.4 18.6 reduce-scatter.1
where the time goes:
time: 151 us
  waiting for transfers between devices  69.4 us (46%)
  matrix products  34.1 us (23%)
  blocking collectives  31.3 us (21%)
  between operations  13.4 us (9%)
  other arithmetic  1.91 us (1%)
    psum x1, waiting for transfers between devices, body(): precond_grad = lax.psum(partial_pre, 'dp')  50.5 us
    psum x1, blocking collectives, body(): grad_total = lax.psum(partial_grad, 'mp')  23 us
    reduce_scatter x1, waiting for transfers between devices, body(): lax.psum_scatter(lax.dot_general(queries, upper_grad, contract, preferred...  18.9 us
    dot_general x1, matrix products, body(): jnp.einsum('lesj,lesc->eljc', right_factor, left_factor, preferred_elemen...  9.26 us
    dot_general x1, matrix products, body(): jnp.einsum('lesd,lkd->lesk', cotangents, project_out, preferred_element_t...  8.75 us
    all_to_all x1, blocking collectives, body(): lax.all_to_all(grad_layer, 'dp', split_axis=1, concat_axis=0, tiled=True)  8.27 us
    dot_general x1, matrix products, body(): lax.dot_general(queries, lower_grad, contract, preferred_element_type=jnp...  6.3 us
    dot_general x1, matrix products, body(): lax.dot_general(queries, upper_grad, contract, preferred_element_type=jnp...  5.65 us
  transfers between devices with their start and end apart: 2, of which 2 were waited for; matrix products, arithmetic and copies ran while one was open for 0% of the time, Pallas kernels for 0%

commit v1 on v0

--- a/solution.py
+++ b/solution.py
@@ -42,7 +42,7 @@
     partial_pre = lax.dot_general(
         spread, preconditioner, contract, preferred_element_type=jnp.float32
     )
-    precond_grad = lax.psum(partial_pre, "dp")
+    precond_grad = jnp.sum(lax.all_gather(partial_pre, "dp"), axis=0)
     upper_grad, lower_grad = split_parts(precond_grad)
     scores = lax.psum_scatter(
         lax.dot_general(queries, upper_grad, contract, preferred_element_type=jnp.float32)

time: 151 us -> 127 us (0.84)
  waiting for transfers between devices: 69.4 us -> 43.9 us
    psum x1 -> x0, waiting for transfers between devices: 50.5 us -> none  [body(): precond_grad = lax.psum(partial_pre, 'dp')]
    all_gather x0 -> x1, waiting for transfers between devices: none -> 24.4 us  [body(): precond_grad = jnp.sum(lax.all_gather(partial_pre, 'dp'), axis=0)]
    reduce_sum x0 -> x1, other arithmetic: none -> 1.72 us  [body(): precond_grad = jnp.sum(lax.all_gather(partial_pre, 'dp'), axis=0)]
where the time goes in v1:
time: 127 us; the launch traced here: 126 us
  waiting for transfers between devices  43.9 us (35%)
  matrix products  34.1 us (27%)
  blocking collectives  31.3 us (25%)
  between operations  13.4 us (11%)
  other arithmetic  2.61 us (2%)
    all_gather x1, waiting for transfers between devices, body(): precond_grad = jnp.sum(lax.all_gather(partial_pre, 'dp'), axis=0)  24.4 us
    psum x1, blocking collectives, body(): grad_total = lax.psum(partial_grad, 'mp')  23 us
    reduce_scatter x1, waiting for transfers between devices, body(): lax.psum_scatter(lax.dot_general(queries, upper_grad, contract, preferred...  19.5 us
    dot_general x1, matrix products, body(): jnp.einsum('lesj,lesc->eljc', right_factor, left_factor, preferred_elemen...  9.26 us
    dot_general x1, matrix products, body(): jnp.einsum('lesd,lkd->lesk', cotangents, project_out, preferred_element_t...  8.75 us
    all_to_all x1, blocking collectives, body(): lax.all_to_all(grad_layer, 'dp', split_axis=1, concat_axis=0, tiled=True)  8.27 us
    dot_general x1, matrix products, body(): lax.dot_general(queries, lower_grad, contract, preferred_element_type=jnp...  6.29 us
    dot_general x1, matrix products, body(): lax.dot_general(queries, upper_grad, contract, preferred_element_type=jnp...  5.65 us
  transfers between devices with their start and end apart: 2, of which 2 were waited for; matrix products, arithmetic and copies ran while one was open for 0% of the time, Pallas kernels for 0%

profile of v1, /device:TPU:0, one launch (start us, length us, event | category | flops | bytes accessed | tf_op | source)
XLA Modules:
  0.0 126.2 jit_solution(11173350082605507123)
XLA Ops:
  6.5 0.0 copy-start
  6.5 0.0 all-gather.3.cloned.1.call-start
  6.5 0.9 broadcast_compare_fusion
  7.4 0.7 copy-done
  8.1 8.8 %fusion.16 = bf16[4,2,256,64]{2,3,0,1:T(8,128)(2,1)S(1)} fusion(bf16[4,64,4096]{2,1,0:T(8,128)(2,1)S(1)} %copy-done, bf16[4,2,256,4096]{3,2,1,0:T(8,128)(2,1)} %param.8, pred[2,256]{1,0:T(4,128)(4,1)S(1)} %broadcast_compare_fusion), kind=kOutput, calls=%fused_computation.8 | convolution fusion | flops 1074003968 | bytes 19137024 | tf_op jit(solution)/shard_map/lesd,lkd->lesk/dot_general | solution.py:28
  16.9 9.3 %fusion.24 = f32[2,4,64,64]{3,2,1,0:T(8,128)S(1)} fusion(bf16[4,2,256,64]{2,3,0,1:T(8,128)(2,1)S(1)} %fusion.16, bf16[4,64,4096]{2,1,0:T(8,128)(2,1)} %param.10, bf16[4,2,256,4096]{3,2,1,0:T(8,128)(2,1)} %param.7), kind=kOutput, calls=%fused_computation.11 | convolution fusion | flops 1090650112 | bytes 19267584 | tf_op jit(solution)/shard_map/lesj,lesc->eljc/dot_general | solution.py:32
  26.2 0.1 reshape.40
  26.3 23.0 %all-reduce.1 = bf16[2,16384]{1,0:T(2,128)(2,1)S(1)} all-reduce(f32[2,16384]{1,0:T(2,128)S(1)} %reshape.40), channel_id=1, replica_groups=mesh['dp'=8,'mp'=4] {'mp'}, use_global_device_ids=true, to_apply=%region_0.1 | all-reduce | flops 32768 | bytes 196608 | tf_op jit(solution)/shard_map/psum | solution.py:36
  49.4 8.3 %all_to_all.19 = bf16[2,8,512]{2,0,1:T(2,128)(2,1)S(1)} all-to-all(bf16[2,8,512]{2,0,1:T(2,128)(2,1)S(1)} %bitcast.29), channel_id=1, replica_groups=mesh['dp'=8,'mp'=4] {'dp'}, dimensions={1} | all-to-all | bytes 32768 | tf_op jit(solution)/shard_map/all_to_all | solution.py:41
  57.7 4.1 %fusion.27 = f32[16,4096]{1,0:T(8,128)} fusion(bf16[16,512]{1,0:T(8,128)(2,1)S(1)} %all_to_all.17, bf16[4096,512]{1,0:T(8,128)(2,1)} %param.12), kind=kOutput, calls=%fused_computation.16 | convolution fusion | flops 67108864 | bytes 4472832 | tf_op jit(solution)/shard_map/dot_general | solution.py:42
  61.8 0.0 all-gather.3.cloned.1.call-update
  61.8 0.0 reduce-scatter.2.cloned.1.call-start
  61.8 24.4 %all-gather.3.cloned.1.call-done = f32[128,4096]{1,0:T(8,128)} async-done(((f32[16,4096]{1,0:T(8,128)}), f32[128,4096]{1,0:T(8,128)}) %all-gather.3.cloned.1.call-update) | async-done | bytes 2097168 | tf_op jit(solution)/shard_map/all_gather | solution.py:45
  86.2 1.7 %reduce_sum.9 = f32[16,4096]{1,0:T(8,128)S(1)} reduce(f32[8,16,4096]{2,1,0:T(8,128)} %bitcast.28, f32[]{:T(128)} %constant.21.clone.1), dimensions={0}, to_apply=%region_1.2 | reduce | flops 458752 | bytes 2359300 | tf_op jit(solution)/shard_map/reduce_sum | solution.py:45
  88.0 5.6 %fusion.28 = f32[16,1024]{1,0:T(8,128)S(1)} fusion(bf16[16,4096]{1,0:T(8,128)(2,1)S(1)} %convert_element_type.21, bf16[1024,4096]{1,0:T(8,128)(2,1)} %param.13), kind=kOutput, calls=%fused_computation.17 | convolution fusion | flops 134217728 | bytes 8585216 | tf_op jit(solution)/shard_map/dot_general | solution.py:48
  93.6 6.3 %fusion.21 = f32[1024,16]{0,1:T(8,128)} fusion(f32[16,1024]{1,0:T(8,128)S(1)} %fusion.28, bf16[1024,4096]{1,0:T(8,128)(2,1)} %param.13, f32[16,4096]{1,0:T(8,128)S(1)} %reduce_sum.9, bf16[16,4096]{1,0:T(8,128)(2,1)S(1)} %convert_element_type.21), kind=kOutput, calls=%fused_computation.10 | convolution fusion | flops 134430720 | bytes 8912896 | tf_op jit(solution)/shard_map/dot_general | solution.py:49
  99.9 0.0 reduce-scatter.2.cloned.1.call-update
  99.9 19.5 %reduce-scatter.2.cloned.1.call-done = f32[256,16]{0,1:T(8,128)} async-done(((f32[1024,16]{0,1:T(8,128)}), f32[256,16]{0,1:T(8,128)}) %reduce-scatter.2.cloned.1.call-update) | async-done | bytes 16400 | tf_op jit(solution)/shard_map/reduce_scatter | solution.py:47
  (4 shorter events, 0.1 us)
Async XLA Ops:
  6.5 1.6 %copy-start = (bf16[4,64,4096]{2,1,0:T(8,128)(2,1)S(1)}, bf16[4,64,4096]{2,1,0:T(8,128)(2,1)}, u32[]{:S(2)}) copy-start(bf16[4,64,4096]{2,1,0:T(8,128)(2,1)} %param.11) | copy-start | bytes 6291460
  6.5 79.7 %all-gather.3.cloned.1.call-start = ((), (), s32[]{:S(2)}) async-start(), calls=%async_computation.3 | async-start | bytes 2359296 | tf_op jit(solution)/shard_map/all_gather | solution.py:45
  61.8 57.6 %reduce-scatter.2.cloned.1.call-start = ((), (), s32[]{:S(2)}) async-start(), calls=%async_computation.2 | async-start | bytes 81920 | tf_op jit(solution)/shard_map/reduce_scatter | solution.py:47
Sparse Core Ops, SparseCore 0:
  61.9 24.2 all-gather.2
  100.1 19.2 reduce-scatter.1
